TPU v7x, 256 devices: a whole 4x4x8 slice. The times are simulated.
256 devices in a mesh: wide: 16 (over z, core), narrow: 16 (over y, x).
Axes of the slice: x: 4, y: 4, z: 8, core: 2. Of those that a mesh axis runs over, the one named last changes fastest.
Arguments:
- screens: bfloat16 [4, 4096, 4096], P(None, 'wide'), may hold values from -3 to 3
- offsets: int32 [2, 128, 4], replicated, may hold values from 0 to 2752, as said below
- valid: int32 [2, 80, 80], P(None, 'narrow'), may hold values from 0 to 1, as said below
- recon: bfloat16 [25600, 5120], P('narrow', 'wide'), may hold values from -0.0390625 to 0.0390625
Outputs:
- slopes: float32 [2, 64, 2, 80, 80], P(None, 'wide', None, 'narrow')
- commands: float32 [64, 5120], P('narrow', 'wide')
Inputs may be any that keep to these rules, and one draw needn't show every extreme that they name: For each coordinate and each layer, the offsets of all items lie within 64 of the smallest, and the largest is exactly 64 above the smallest. In the 5 subaperture rows of one index of narrow, each sensor has at most 300 valid subapertures; in every draw one index of narrow holds exactly 300 for each sensor.
All inputs are finite; a program needn't handle non-finite values.
Results may differ from a plain program's by a relative error of at most 0.0043.
Values may be sent and summed in bfloat16 or wider, within the bound.
No kernel may reach another device: no remote copies, remote signals or barrier semaphores. Data moves between devices by JAX's collectives and lax.ppermute only.
A program may use at most 128 MiB of HBM per device.

v0:
```python
import math
import jax
import jax.numpy as jnp
from jax import lax
from jax.sharding import PartitionSpec as P

L = 4
NSUB = 80
SAMP = 16
NPIX = 32
NSENS = 2
SPREAD = 64
FR_DEV = 4
PUP = 1280


def broadcast(block, axis, source):
    block = jnp.where(lax.axis_index(axis) == source, block, jnp.zeros_like(block))
    return lax.psum(block, axis)


def dft_table(samp, npix):
    sample_ids = jnp.arange(samp * samp, dtype=jnp.int32)
    pixel_ids = jnp.arange(npix * npix, dtype=jnp.int32)
    sample_row = sample_ids // samp
    sample_col = sample_ids % samp
    pixel_row = pixel_ids // npix - npix // 2
    pixel_col = pixel_ids % npix - npix // 2
    phase_turns = jnp.mod(
        sample_row[:, None] * pixel_row[None, :] + sample_col[:, None] * pixel_col[None, :], npix
    )
    angles = phase_turns.astype(jnp.float32) * jnp.float32(-2.0 * math.pi / npix)
    cosine = jnp.cos(angles).astype(jnp.bfloat16)
    sine_part = jnp.sin(angles).astype(jnp.bfloat16)
    top_rows = jnp.concatenate([cosine, sine_part], axis=1)
    bottom_rows = jnp.concatenate([-sine_part, cosine], axis=1)
    return jnp.concatenate([top_rows, bottom_rows], axis=0)


def subaperture_fields(pupil_phase, samp):
    sub_rows = pupil_phase.shape[0] // samp
    sub_cols = pupil_phase.shape[1] // samp
    samples = (
        pupil_phase.reshape(sub_rows, samp, sub_cols, samp)
        .transpose(0, 2, 1, 3)
        .reshape(sub_rows * sub_cols, samp * samp)
    )
    return jnp.concatenate([jnp.cos(samples), jnp.sin(samples)], axis=1).astype(jnp.bfloat16)


def centroids(fields, transform, npix):
    spectrum = jnp.dot(fields, transform, preferred_element_type=jnp.float32)
    pixel_count = npix * npix
    real_part = spectrum[:, :pixel_count]
    imag_part = spectrum[:, pixel_count:]
    intensity = real_part * real_part + imag_part * imag_part
    pixel_ids = jnp.arange(pixel_count, dtype=jnp.int32)
    along_x = (pixel_ids % npix - npix // 2).astype(jnp.float32)
    along_y = (pixel_ids // npix - npix // 2).astype(jnp.float32)
    flux_total = jnp.sum(intensity, axis=1)
    centre_x = jnp.sum(intensity * along_x[None, :], axis=1) / flux_total
    centre_y = jnp.sum(intensity * along_y[None, :], axis=1) / flux_total
    return jnp.stack([centre_x, centre_y], axis=1)


def cut_windows(rows_block, row_first, col_first, pixel_rows):

    def cut_one(row_at, col_at):
        return lax.dynamic_slice(rows_block, (row_at, col_at), (pixel_rows, PUP))

    return jax.vmap(cut_one)(row_first, col_first).astype(jnp.float32)


def body(screens, offsets, valid, recon):
    wide_count = lax.axis_size("wide")
    wide_index = lax.axis_index("wide")
    narrow_index = lax.axis_index("narrow")
    band_rows = screens.shape[1]
    sub_rows = valid.shape[1]
    pixel_rows = sub_rows * SAMP
    union_cols = PUP + SPREAD
    local_items = FR_DEV * NSENS
    own_offsets = lax.dynamic_slice_in_dim(offsets, wide_index * local_items, local_items, 1)
    lowest = jnp.min(offsets, axis=1)
    band_blocks = [
        lax.dynamic_slice_in_dim(screens[which_layer], lowest[1, which_layer], union_cols, 1)
        for which_layer in range(L)
    ]
    pupil_phase = jnp.zeros((local_items, pixel_rows, PUP), jnp.float32)
    for which_layer in range(L):
        group_start = lowest[0, which_layer] + pixel_rows * narrow_index
        root_upper = group_start // band_rows
        root_lower = jnp.minimum(root_upper + 1, wide_count - 1)
        upper_rows = broadcast(band_blocks[which_layer], "wide", root_upper)
        lower_rows = broadcast(band_blocks[which_layer], "wide", root_lower)
        joined_rows = jnp.concatenate([upper_rows, lower_rows], axis=0)
        row_first = (
            own_offsets[0, :, which_layer] + pixel_rows * narrow_index - root_upper * band_rows
        )
        col_first = own_offsets[1, :, which_layer] - lowest[1, which_layer]
        pupil_phase = pupil_phase + cut_windows(joined_rows, row_first, col_first, pixel_rows)
    transform = dft_table(SAMP, NPIX)
    frame_phase = pupil_phase.reshape(FR_DEV, NSENS, pixel_rows, PUP)
    valid_flags = valid.reshape(-1)

    def frame_fields(frame_block):
        return jnp.concatenate(
            [subaperture_fields(frame_block[sensor_index], SAMP) for sensor_index in range(NSENS)],
            axis=0,
        )

    def one_frame(frame_block):
        return centroids(frame_fields(frame_block), transform, NPIX) * valid_flags[:, None].astype(
            jnp.float32
        )

    measured = lax.map(one_frame, frame_phase)
    measured = measured.reshape(FR_DEV, NSENS, sub_rows, NSUB, 2)
    slopes = measured.transpose(4, 0, 1, 2, 3)
    slope_vector = (
        measured.transpose(0, 2, 1, 3, 4)
        .reshape(FR_DEV, sub_rows * NSENS * NSUB * 2)
        .astype(jnp.bfloat16)
    )
    partial_commands = jnp.dot(
        lax.all_gather(slope_vector, "wide", axis=0, tiled=True),
        recon,
        preferred_element_type=jnp.float32,
    )
    commands = lax.psum_scatter(partial_commands, "narrow", scatter_dimension=0, tiled=True)
    return (slopes, commands)


def solution(mesh):
    return jax.shard_map(
        body,
        mesh=mesh,
        in_specs=(P(None, "wide", None), P(), P(None, "narrow", None), P("narrow", "wide")),
        out_specs=(P(None, "wide", None, "narrow", None), P("narrow", "wide")),
        check_vma=False,
    )
```

profile of v0, /device:TPU:32, one launch (start us, length us, event | category | flops | bytes accessed | tf_op | source)
XLA Modules:
  0.0 496.8 jit_solution(6549098456706438841)
XLA Ops:
  16.5 5.7 %fusion.54 = (bf16[1,256,4096]{2,1,0:T(8,128)(2,1)}, bf16[1,256,4096]{2,1,0:T(8,128)(2,1)}, bf16[1,256,4096]{2,1,0:T(8,128)(2,1)S(1)}, bf16[1,256,4096]{2,1,0:T(8,128)(2,1)}) fusion(bf16[4,256,4096]{2,1,0:T(8,128)(2,1)} %param.6), kind=kLoop, calls=%fused_computation.126 | loop fusion | bytes 16777216 | tf_op jit(solution)/shard_map/slice | solution.py:86
  24.7 4.1 select_bitcast_fusion.5
  28.8 3.9 select_bitcast_fusion.1
  33.4 2.6 compare_select_fusion.7
  36.1 4.3 fusion.48
  40.4 4.6 sine_convert_fusion.2
  46.6 113.5 %all-reduce.7.cloned.1.call-done = (bf16[256,1344]{1,0:T(8,128)(2,1)}, bf16[256,1344]{1,0:T(8,128)(2,1)}, bf16[256,1344]{1,0:T(8,128)(2,1)}, bf16[256,1344]{1,0:...) async-done(((bf16[256,1344]{1,0:T(8,128)(2,1)}, bf16[256,1344]{1,0:T(8,128)(2,1)}, ...) | async-done | bytes 5505040 | tf_op jit(solution)/shard_map/psum | solution.py:19
  160.1 2.6 pad_maximum_fusion
  162.9 24.3 %while.18 = (s32[]{:T(128)}, bf16[512,1344]{1,0:T(8,128)(2,1)}, s32[8,2]{0,1:T(2,128)S(1)}, bf16[8,80,1280]{2,1,0:T(8,128)(2,1)S(1)}, s32[]{:T(128)}) while((s32[]{:T(128)}, bf16[512,1344]{1,0:T(8,128)(2,1)}, s32[8,2]{0,1:T(2,128)S(1)}, bf16[8,80,1280]{2,1,0:T(8,128)(2,1)S(1)}, s32[]{:T(128)}) %tuple.146), condition=%wide.while_cond, body=%wide.while_body.sunk | while | flops 2 | bytes 409709 | solution.py:69
  163.5 2.4 bitcast_dynamic-update-slice_fusion.8
  166.6 2.4 bitcast_dynamic-update-slice_fusion.8
  169.6 2.4 bitcast_dynamic-update-slice_fusion.8
  172.7 2.4 bitcast_dynamic-update-slice_fusion.8
  175.7 2.4 bitcast_dynamic-update-slice_fusion.8
  178.8 2.4 bitcast_dynamic-update-slice_fusion.8
  181.8 2.4 bitcast_dynamic-update-slice_fusion.8
  184.9 2.4 bitcast_dynamic-update-slice_fusion.8
  187.2 2.9 pad_maximum_fusion.1
  191.5 28.6 %while.19 = (s32[]{:T(128)}, bf16[512,1344]{1,0:T(8,128)(2,1)}, s32[8,2]{0,1:T(2,128)S(1)}, bf16[8,80,1280]{2,1,0:T(8,128)(2,1)}, s32[]{:T(128)}) while((s32[]{:T(128)}, bf16[512,1344]{1,0:T(8,128)(2,1)}, s32[8,2]{0,1:T(2,128)S(1)}, bf16[8,80,1280]{2,1,0:T(8,128)(2,1)}, s32[]{:T(128)}) %tuple.143), condition=%wide.while_cond.1, body=%wide.while_body.1.sunk | while | flops 2 | bytes 411233 | solution.py:69
  192.1 3.0 bitcast_dynamic-update-slice_fusion.9
  195.7 3.0 bitcast_dynamic-update-slice_fusion.9
  199.3 3.0 bitcast_dynamic-update-slice_fusion.9
  202.8 3.0 bitcast_dynamic-update-slice_fusion.9
  206.4 3.0 bitcast_dynamic-update-slice_fusion.9
  210.0 3.0 bitcast_dynamic-update-slice_fusion.9
  213.5 3.0 bitcast_dynamic-update-slice_fusion.9
  217.2 3.0 bitcast_dynamic-update-slice_fusion.9
  220.1 2.4 pad_maximum_fusion.2
  222.6 23.4 %while.20 = (s32[]{:T(128)}, bf16[512,1344]{1,0:T(8,128)(2,1)}, s32[8,2]{0,1:T(2,128)S(1)}, bf16[8,80,1280]{2,1,0:T(8,128)(2,1)S(1)}, s32[]{:T(128)}) while((s32[]{:T(128)}, bf16[512,1344]{1,0:T(8,128)(2,1)}, s32[8,2]{0,1:T(2,128)S(1)}, bf16[8,80,1280]{2,1,0:T(8,128)(2,1)S(1)}, s32[]{:T(128)}) %tuple.140), condition=%wide.while_cond.2, body=%wide.while_body.2.sunk | while | flops 2 | bytes 409709 | solution.py:69
  223.3 2.3 bitcast_dynamic-update-slice_fusion.10
  226.2 2.3 bitcast_dynamic-update-slice_fusion.10
  229.1 2.3 bitcast_dynamic-update-slice_fusion.10
  232.1 2.3 bitcast_dynamic-update-slice_fusion.10
  235.0 2.3 bitcast_dynamic-update-slice_fusion.10
  237.9 2.3 bitcast_dynamic-update-slice_fusion.10
  240.8 2.3 bitcast_dynamic-update-slice_fusion.10
  243.8 2.3 bitcast_dynamic-update-slice_fusion.10
  246.1 2.9 pad_maximum_fusion.3
  249.0 24.1 %while.21 = (s32[]{:T(128)}, bf16[512,1344]{1,0:T(8,128)(2,1)}, s32[8,2]{0,1:T(2,128)S(1)}, bf16[8,80,1280]{2,1,0:T(8,128)(2,1)S(1)}, s32[]{:T(128)}) while((s32[]{:T(128)}, bf16[512,1344]{1,0:T(8,128)(2,1)}, s32[8,2]{0,1:T(2,128)S(1)}, bf16[8,80,1280]{2,1,0:T(8,128)(2,1)S(1)}, s32[]{:T(128)}) %tuple.137), condition=%wide.while_cond.3, body=%wide.while_body.3.sunk | while | flops 2 | bytes 409709 | solution.py:69
  249.7 2.3 bitcast_dynamic-update-slice_fusion.11
  252.7 2.3 bitcast_dynamic-update-slice_fusion.11
  255.7 2.3 bitcast_dynamic-update-slice_fusion.11
  258.8 2.3 bitcast_dynamic-update-slice_fusion.11
  261.8 2.3 bitcast_dynamic-update-slice_fusion.11
  264.8 2.3 bitcast_dynamic-update-slice_fusion.11
  267.8 2.3 bitcast_dynamic-update-slice_fusion.11
  270.8 2.3 bitcast_dynamic-update-slice_fusion.11
  273.2 4.9 convert_add_fusion
  278.1 98.5 %while.17 = (s32[]{:T(128)}, f32[4,800,2]{1,2,0:T(2,128)S(1)}, f32[4,2,80,1280]{3,2,1,0:T(8,128)}, bf16[512,2048]{1,0:T(8,128)(2,1)}, f32[800,1]{0,1:T(1,128)S(1)}, /*index=5*/s32[]{:T(128)}, s32[]{:T(128)}, s32[]{}, f32[]{:T(128)}) while((s32[]{:T(128)}, f32[4,800,2]{1,2,0:T(2,128)S(1)}, f32[4,2,80,1280]{3,2,1,0:T(8,128)}, ...), condition=%wide.region_13.14_spmd, body=%wide.region_9.13_spmd.sunk | while | flops 1687980416 | bytes 22656888 | solution.py:117
  278.1 5.2 %cosine_convert_fusion.4 = (bf16[1,1,80,1280]{3,2,1,0:T(8,128)(2,1)}, bf16[1,1,80,1280]{3,2,1,0:T(8,128)(2,1)}, bf16[1,1,80,1280]{3,2,1,0:T(8,128)(2,1)S(1)}, bf16[1,1,80,1280]{3,2,1,0:T(8,128)(2,1)S(1)}) fusion(f32[4,2,80,1280]{3,2,1,0:T(8,128)} %get-tuple-element.498, s32[]{:T(128)} %get-tuple-element.487, s32[]{:T(128)S(6)} %add.480), kind=kLoop, calls=%fused_computation.24.clone.1 | loop fusion | flops 409600 | bytes 1638408 | tf_op jit(solution)/shard_map/convert.15
  286.5 2.2 cos.49
  290.8 2.2 sin.47
  297.6 3.9 fusion.73
  302.7 5.2 %cosine_convert_fusion.4 = (bf16[1,1,80,1280]{3,2,1,0:T(8,128)(2,1)}, bf16[1,1,80,1280]{3,2,1,0:T(8,128)(2,1)}, bf16[1,1,80,1280]{3,2,1,0:T(8,128)(2,1)S(1)}, bf16[1,1,80,1280]{3,2,1,0:T(8,128)(2,1)S(1)}) fusion(f32[4,2,80,1280]{3,2,1,0:T(8,128)} %get-tuple-element.498, s32[]{:T(128)} %get-tuple-element.487, s32[]{:T(128)S(6)} %add.480), kind=kLoop, calls=%fused_computation.24.clone.1 | loop fusion | flops 409600 | bytes 1638408 | tf_op jit(solution)/shard_map/convert.15
  311.2 2.2 cos.49
  322.2 3.8 fusion.73
  327.3 5.2 %cosine_convert_fusion.4 = (bf16[1,1,80,1280]{3,2,1,0:T(8,128)(2,1)}, bf16[1,1,80,1280]{3,2,1,0:T(8,128)(2,1)}, bf16[1,1,80,1280]{3,2,1,0:T(8,128)(2,1)S(1)}, bf16[1,1,80,1280]{3,2,1,0:T(8,128)(2,1)S(1)}) fusion(f32[4,2,80,1280]{3,2,1,0:T(8,128)} %get-tuple-element.498, s32[]{:T(128)} %get-tuple-element.487, s32[]{:T(128)S(6)} %add.480), kind=kLoop, calls=%fused_computation.24.clone.1 | loop fusion | flops 409600 | bytes 1638408 | tf_op jit(solution)/shard_map/convert.15
  335.8 2.2 cos.49
  340.0 2.2 sin.47
  346.8 3.9 fusion.73
  351.9 5.2 %cosine_convert_fusion.4 = (bf16[1,1,80,1280]{3,2,1,0:T(8,128)(2,1)}, bf16[1,1,80,1280]{3,2,1,0:T(8,128)(2,1)}, bf16[1,1,80,1280]{3,2,1,0:T(8,128)(2,1)S(1)}, bf16[1,1,80,1280]{3,2,1,0:T(8,128)(2,1)S(1)}) fusion(f32[4,2,80,1280]{3,2,1,0:T(8,128)} %get-tuple-element.498, s32[]{:T(128)} %get-tuple-element.487, s32[]{:T(128)S(6)} %add.480), kind=kLoop, calls=%fused_computation.24.clone.1 | loop fusion | flops 409600 | bytes 1638408 | tf_op jit(solution)/shard_map/convert.15
  371.5 3.9 fusion.73
  377.3 18.1 %all-gather = bf16[16,4,1600]{2,1,0:T(4,128)(2,1)S(1)} all-gather(bf16[1,4,1600]{2,1,0:T(4,128)(2,1)S(1)} %copy.28), channel_id=1, replica_groups=mesh['wide'=16,'narrow'=16] {'wide'}, dimensions={0}, use_global_device_ids=true | all-gather | bytes 217600 | tf_op jit(solution)/shard_map/all_gather | solution.py:126
  398.5 90.2 %all-reduce.5.cloned.1.call-done = f32[64,320]{1,0:T(8,128)} async-done(((f32[64,320]{1,0:T(8,128)}), f32[64,320]{1,0:T(8,128)}) %all-reduce.5.cloned.1.call-update) | async-done | bytes 81936
  (181 shorter events, 81.5 us)
Async XLA Ops:
  7.2 388.3 %copy-start = (bf16[1600,320]{0,1:T(8,128)(2,1)S(1)}, bf16[1600,320]{0,1:T(8,128)(2,1)}, u32[]{:S(2)}) copy-start(bf16[1600,320]{0,1:T(8,128)(2,1)} %param.9) | copy-start | bytes 3072004
  7.2 152.9 %all-reduce.7.cloned.1.call-start = ((), (), s32[]{:S(2)}) async-start(), calls=%async_computation.1 | async-start | bytes 11534336 | tf_op jit(solution)/shard_map/psum | solution.py:19
  32.6 0.7 copy-start.7
  32.6 0.8 copy-start.6
  32.7 456.0 %all-reduce.5.cloned.1.call-start = ((), (), s32[]{:S(2)}) async-start(), calls=%async_computation | async-start | bytes 196608
  162.7 24.5 %copy-start.5 = (bf16[256,1344]{1,0:T(8,128)(2,1)S(1)}, bf16[256,1344]{1,0:T(8,128)(2,1)}, u32[]{:S(2)}) copy-start(bf16[256,1344]{1,0:T(8,128)(2,1)} %get-tuple-element.187) | copy-start | bytes 2064388
  187.2 4.3 copy-start.1
  190.2 29.9 %copy-start.4 = (bf16[256,1344]{1,0:T(8,128)(2,1)S(1)}, bf16[256,1344]{1,0:T(8,128)(2,1)}, u32[]{:S(2)}) copy-start(bf16[256,1344]{1,0:T(8,128)(2,1)} %get-tuple-element.185) | copy-start | bytes 2064388
  222.5 23.5 %copy-start.3 = (bf16[256,1344]{1,0:T(8,128)(2,1)S(1)}, bf16[256,1344]{1,0:T(8,128)(2,1)}, u32[]{:S(2)}) copy-start(bf16[256,1344]{1,0:T(8,128)(2,1)} %get-tuple-element.183) | copy-start | bytes 2064388
  246.0 2.9 copy-start.2
  376.5 20.1 %copy-start.8 = (u32[256]{0:T(256)S(1)}, u32[256]{0:T(256)}, u32[]{:S(2)}) copy-start(u32[256]{0:T(256)} %constant.269) | copy-start | bytes 3076
Sparse Core Ops, SparseCore 0:
  32.8 127.2 all-reduce.6
  396.7 91.9 all-reduce.4
where the time goes:
time: 500 us; the launch traced here: 497 us
  waiting for transfers between devices  204 us (41%)
  local copies, waits for them, and re-layouts  169 us (34%)
  other arithmetic  63.1 us (13%)
  between operations  25.2 us (5%)
  blocking collectives  18.1 us (4%)
  matrix products  16.5 us (3%)
    psum x1, waiting for transfers between devices, broadcast(): return lax.psum(block, axis)  114 us
    gather x96, local copies, waits for them, and re-layouts  100 us
    unnamed x3, waiting for transfers between devices  90.2 us
    cos x24, local copies, waits for them, and re-layouts, subaperture_fields(): jnp.cos(samples)  29.9 us
    sin x24, local copies, waits for them, and re-layouts, subaperture_fields(): jnp.sin(samples)  27.2 us
    another operation x8, other arithmetic  20.9 us
    all_gather x1, blocking collectives, body(): lax.all_gather(slope_vector, 'wide', axis=0, tiled=True)  18.1 us
    dot_general x4, matrix products, centroids(): spectrum = jnp.dot(fields, transform, preferred_element_type=jnp.float32)  15.4 us
  transfers between devices with their start and end apart: 2, of which 2 were waited for; matrix products, arithmetic and copies ran while one was open for 3% of the time, Pallas kernels for 0%

commit v1 on v0

--- a/solution.py
+++ b/solution.py
@@ -16,7 +16,12 @@
 
 def broadcast(block, axis, source):
     block = jnp.where(lax.axis_index(axis) == source, block, jnp.zeros_like(block))
-    return lax.psum(block, axis)
+
+    def grid_replace(x_local):
+        moved = lax.all_gather(x_local, axis_name=axis).sum(axis=0)
+        return moved
+
+    return grid_replace(block)
 
 
 def dft_table(samp, npix):

time: 500 us -> 862 us (1.72)
  waiting for transfers between devices: 204 us -> 493 us
  other arithmetic: 63.1 us -> 107 us
  local copies, waits for them, and re-layouts: 169 us -> 194 us
    all_gather x0 -> x8, waiting for transfers between devices: none -> 400 us  [grid_replace(): moved = lax.all_gather(x_local, axis_name=axis).sum(axis=0)]
    psum x1 -> x0, waiting for transfers between devices: 114 us -> none  [broadcast(): return lax.psum(block, axis)]
    reduce_sum x0 -> x8, other arithmetic: none -> 51.1 us  [grid_replace(): moved = lax.all_gather(x_local, axis_name=axis).sum(axis=0)]
    unnamed x27 -> x29, local copies, waits for them, and re-layouts: 5.09 us -> 18.2 us
    unnamed x3 -> x10, waiting for transfers between devices: 90.2 us -> 93.7 us
  transfers between devices with their start and end apart: 2 -> 9, of which waited for: 2 -> 8; matrix products, arithmetic and copies ran while one was open for 3% -> 19% of each run, Pallas kernels for 0% -> 0%
where the time goes in v1:
time: 862 us; the launch traced here: 855 us
  waiting for transfers between devices  493 us (57%)
  local copies, waits for them, and re-layouts  194 us (23%)
  other arithmetic  107 us (12%)
  between operations  25.4 us (3%)
  blocking collectives  17.1 us (2%)
  matrix products  16.5 us (2%)
    all_gather x8, waiting for transfers between devices, grid_replace(): moved = lax.all_gather(x_local, axis_name=axis).sum(axis=0)  400 us
    gather x96, local copies, waits for them, and re-layouts  105 us
    unnamed x10, waiting for transfers between devices  93.7 us
    reduce_sum x8, other arithmetic, grid_replace(): moved = lax.all_gather(x_local, axis_name=axis).sum(axis=0)  51.1 us
    cos x24, local copies, waits for them, and re-layouts, subaperture_fields(): jnp.cos(samples)  30 us
    sin x24, local copies, waits for them, and re-layouts, subaperture_fields(): jnp.sin(samples)  27 us
    another operation x8, other arithmetic  20.9 us
    unnamed x29, local copies, waits for them, and re-layouts  18.2 us
  transfers between devices with their start and end apart: 9, of which 8 were waited for; matrix products, arithmetic and copies ran while one was open for 19% of the time, Pallas kernels for 0%

profile of v1, /device:TPU:32, one launch (start us, length us, event | category | flops | bytes accessed | tf_op | source)
XLA Modules:
  0.0 854.8 jit_solution(10217909437146179752)
XLA Ops:
  12.1 5.7 fusion.54
  19.0 3.4 constant_dynamic-slice_fusion.11
  24.6 2.3 broadcast_select_fusion.7
  30.7 2.3 broadcast_select_fusion.5
  38.1 3.2 constant_dynamic-slice_fusion.9
  48.1 2.6 compare_select_fusion.7
  50.8 4.3 fusion.48
  55.1 4.6 sine_convert_fusion.2
  61.2 34.9 %all-gather.10.cloned.1.call-done = bf16[16,256,1344]{1,2,0:T(8,128)(2,1)} async-done(((bf16[1,256,1344]{1,2,0:T(8,128)(2,1)}), bf16[16,256,1344]{1,2,0:T(8,128)(2,1)}) %all-gather.10.cloned.1.call-update) | async-done | bytes 11010064 | tf_op jit(solution)/shard_map/all_gather | solution.py:21
  96.1 6.1 reduce_sum.135
  102.2 62.6 %all-gather.12.cloned.1.call-done = bf16[16,256,1344]{1,2,0:T(8,128)(2,1)} async-done(((bf16[1,256,1344]{1,2,0:T(8,128)(2,1)}), bf16[16,256,1344]{1,2,0:T(8,128)(2,1)}) %all-gather.12.cloned.1.call-update) | async-done | bytes 11010064 | tf_op jit(solution)/shard_map/all_gather | solution.py:21
  164.8 6.7 reduce_sum.136
  174.3 59.2 %all-gather.14.cloned.1.call-done = bf16[16,256,1344]{1,2,0:T(8,128)(2,1)} async-done(((bf16[1,256,1344]{1,2,0:T(8,128)(2,1)}), bf16[16,256,1344]{1,2,0:T(8,128)(2,1)}) %all-gather.14.cloned.1.call-update) | async-done | bytes 11010064 | tf_op jit(solution)/shard_map/all_gather | solution.py:21
  233.5 6.1 reduce_sum.137
  239.5 62.4 %all-gather.16.cloned.1.call-done = bf16[16,256,1344]{1,2,0:T(8,128)(2,1)} async-done(((bf16[1,256,1344]{1,2,0:T(8,128)(2,1)}), bf16[16,256,1344]{1,2,0:T(8,128)(2,1)}) %all-gather.16.cloned.1.call-update) | async-done | bytes 11010064 | tf_op jit(solution)/shard_map/all_gather | solution.py:21
  302.0 6.7 reduce_sum.138
  311.6 58.9 %all-gather.18.cloned.1.call-done = bf16[16,256,1344]{1,2,0:T(8,128)(2,1)} async-done(((bf16[1,256,1344]{1,2,0:T(8,128)(2,1)}), bf16[16,256,1344]{1,2,0:T(8,128)(2,1)}) %all-gather.18.cloned.1.call-update) | async-done | bytes 11010064 | tf_op jit(solution)/shard_map/all_gather | solution.py:21
  370.5 6.1 reduce_sum.139
  376.6 62.4 %all-gather.20.cloned.1.call-done = bf16[16,256,1344]{1,2,0:T(8,128)(2,1)} async-done(((bf16[1,256,1344]{1,2,0:T(8,128)(2,1)}), bf16[16,256,1344]{1,2,0:T(8,128)(2,1)}) %all-gather.20.cloned.1.call-update) | async-done | bytes 11010064 | tf_op jit(solution)/shard_map/all_gather | solution.py:21
  439.0 6.7 reduce_sum.140
  448.5 59.2 %all-gather.22.cloned.1.call-done = bf16[16,256,1344]{1,2,0:T(8,128)(2,1)} async-done(((bf16[1,256,1344]{1,2,0:T(8,128)(2,1)}), bf16[16,256,1344]{1,2,0:T(8,128)(2,1)}) %all-gather.22.cloned.1.call-update) | async-done | bytes 11010064 | tf_op jit(solution)/shard_map/all_gather | solution.py:21
  507.7 6.1 reduce_sum.141
  513.8 23.0 %while.18 = (s32[]{:T(128)}, bf16[512,1344]{1,0:T(8,128)(2,1)}, s32[8,2]{0,1:T(2,128)S(1)}, bf16[8,80,1280]{2,1,0:T(8,128)(2,1)S(1)}, s32[]{:T(128)}) while((s32[]{:T(128)}, bf16[512,1344]{1,0:T(8,128)(2,1)}, s32[8,2]{0,1:T(2,128)S(1)}, bf16[8,80,1280]{2,1,0:T(8,128)(2,1)S(1)}, s32[]{:T(128)}) %tuple.149), condition=%wide.while_cond, body=%wide.while_body.sunk | while | flops 2 | bytes 409709 | solution.py:74
  531.7 2.3 bitcast_dynamic-update-slice_fusion.8
  538.2 29.9 %while.19 = (s32[]{:T(128)}, bf16[512,1344]{1,0:T(8,128)(2,1)}, s32[8,2]{0,1:T(2,128)S(1)}, bf16[8,80,1280]{2,1,0:T(8,128)(2,1)}, s32[]{:T(128)}) while((s32[]{:T(128)}, bf16[512,1344]{1,0:T(8,128)(2,1)}, s32[8,2]{0,1:T(2,128)S(1)}, bf16[8,80,1280]{2,1,0:T(8,128)(2,1)}, s32[]{:T(128)}) %tuple.146), condition=%wide.while_cond.1, body=%wide.while_body.1.sunk | while | flops 2 | bytes 411233 | solution.py:74
  538.9 3.1 bitcast_dynamic-update-slice_fusion.9
  542.6 3.1 bitcast_dynamic-update-slice_fusion.9
  546.4 3.1 bitcast_dynamic-update-slice_fusion.9
  550.1 3.1 bitcast_dynamic-update-slice_fusion.9
  553.8 3.1 bitcast_dynamic-update-slice_fusion.9
  557.6 3.1 bitcast_dynamic-update-slice_fusion.9
  561.3 3.1 bitcast_dynamic-update-slice_fusion.9
  565.0 3.1 bitcast_dynamic-update-slice_fusion.9
  569.4 29.0 %while.20 = (s32[]{:T(128)}, bf16[512,1344]{1,0:T(8,128)(2,1)}, s32[8,2]{0,1:T(2,128)S(1)}, bf16[8,80,1280]{2,1,0:T(8,128)(2,1)}, s32[]{:T(128)}) while((s32[]{:T(128)}, bf16[512,1344]{1,0:T(8,128)(2,1)}, s32[8,2]{0,1:T(2,128)S(1)}, bf16[8,80,1280]{2,1,0:T(8,128)(2,1)}, s32[]{:T(128)}) %tuple.143), condition=%wide.while_cond.2, body=%wide.while_body.2.sunk | while | flops 2 | bytes 411233 | solution.py:74
  570.1 3.0 bitcast_dynamic-update-slice_fusion.10
  573.7 3.0 bitcast_dynamic-update-slice_fusion.10
  577.3 3.0 bitcast_dynamic-update-slice_fusion.10
  580.9 3.0 bitcast_dynamic-update-slice_fusion.10
  584.6 3.0 bitcast_dynamic-update-slice_fusion.10
  588.2 3.0 bitcast_dynamic-update-slice_fusion.10
  591.8 3.0 bitcast_dynamic-update-slice_fusion.10
  595.4 3.0 bitcast_dynamic-update-slice_fusion.10
  598.4 6.7 reduce_sum.142
  608.0 23.3 %while.21 = (s32[]{:T(128)}, bf16[512,1344]{1,0:T(8,128)(2,1)}, s32[8,2]{0,1:T(2,128)S(1)}, bf16[8,80,1280]{2,1,0:T(8,128)(2,1)S(1)}, s32[]{:T(128)}) while((s32[]{:T(128)}, bf16[512,1344]{1,0:T(8,128)(2,1)}, s32[8,2]{0,1:T(2,128)S(1)}, bf16[8,80,1280]{2,1,0:T(8,128)(2,1)S(1)}, s32[]{:T(128)}) %tuple.140), condition=%wide.while_cond.3, body=%wide.while_body.3.sunk | while | flops 2 | bytes 409709 | solution.py:74
  608.6 2.3 bitcast_dynamic-update-slice_fusion.11
  611.5 2.3 bitcast_dynamic-update-slice_fusion.11
  614.4 2.3 bitcast_dynamic-update-slice_fusion.11
  617.4 2.3 bitcast_dynamic-update-slice_fusion.11
  620.3 2.3 bitcast_dynamic-update-slice_fusion.11
  623.2 2.3 bitcast_dynamic-update-slice_fusion.11
  626.1 2.3 bitcast_dynamic-update-slice_fusion.11
  629.0 2.3 bitcast_dynamic-update-slice_fusion.11
  631.3 4.8 convert_add_fusion
  636.1 98.5 %while.17 = (s32[]{:T(128)}, f32[4,800,2]{1,2,0:T(2,128)S(1)}, f32[4,2,80,1280]{3,2,1,0:T(8,128)}, bf16[512,2048]{1,0:T(8,128)(2,1)}, f32[800,1]{0,1:T(1,128)S(1)}, /*index=5*/s32[]{:T(128)}, s32[]{:T(128)}, s32[]{}, f32[]{:T(128)}) while((s32[]{:T(128)}, f32[4,800,2]{1,2,0:T(2,128)S(1)}, f32[4,2,80,1280]{3,2,1,0:T(8,128)}, ...), condition=%wide.region_13.14_spmd, body=%wide.region_9.13_spmd.sunk | while | flops 1687980416 | bytes 22656888 | solution.py:122
  636.3 5.2 cosine_convert_fusion.4
  655.8 3.9 fusion.73
  660.9 5.2 cosine_convert_fusion.4
  680.4 3.9 fusion.73
  685.5 5.2 cosine_convert_fusion.4
  705.0 3.9 fusion.73
  710.1 5.2 cosine_convert_fusion.4
  729.6 3.9 fusion.73
  735.4 17.1 %all-gather = bf16[16,4,1600]{2,1,0:T(4,128)(2,1)S(1)} all-gather(bf16[1,4,1600]{2,1,0:T(4,128)(2,1)S(1)} %copy.48), channel_id=1, replica_groups=mesh['wide'=16,'narrow'=16] {'wide'}, dimensions={0}, use_global_device_ids=true | all-gather | bytes 217600 | tf_op jit(solution)/shard_map/all_gather | solution.py:131
  755.6 91.1 %all-reduce.3.cloned.1.call-done = f32[64,320]{1,0:T(8,128)} async-done(((f32[64,320]{1,0:T(8,128)}), f32[64,320]{1,0:T(8,128)}) %all-reduce.3.cloned.1.call-update) | async-done | bytes 81936
  (216 shorter events, 131.1 us)
Async XLA Ops:
  7.2 745.4 %copy-start = (bf16[1600,320]{0,1:T(8,128)(2,1)S(1)}, bf16[1600,320]{0,1:T(8,128)(2,1)}, u32[]{:S(2)}) copy-start(bf16[1600,320]{0,1:T(8,128)(2,1)} %param.9) | copy-start | bytes 3072004
  7.2 89.0 %all-gather.10.cloned.1.call-start = ((), (), s32[]{:S(2)}) async-start(), calls=%async_computation | async-start | bytes 11698176 | tf_op jit(solution)/shard_map/all_gather | solution.py:21
  27.0 137.8 %all-gather.12.cloned.1.call-start = ((), (), s32[]{:S(2)}) async-start(), calls=%async_computation.1 | async-start | bytes 11698176 | tf_op jit(solution)/shard_map/all_gather | solution.py:21
  27.7 205.7 %all-gather.14.cloned.1.call-start = ((), (), s32[]{:S(2)}) async-start(), calls=%async_computation.2 | async-start | bytes 11698176 | tf_op jit(solution)/shard_map/all_gather | solution.py:21
  33.0 269.0 %all-gather.16.cloned.1.call-start = ((), (), s32[]{:S(2)}) async-start(), calls=%async_computation.3 | async-start | bytes 11698176 | tf_op jit(solution)/shard_map/all_gather | solution.py:21
  33.6 336.9 %all-gather.18.cloned.1.call-start = ((), (), s32[]{:S(2)}) async-start(), calls=%async_computation.4 | async-start | bytes 11698176 | tf_op jit(solution)/shard_map/all_gather | solution.py:21
  42.7 2.5 copy-start.2
  43.8 395.2 %all-gather.20.cloned.1.call-start = ((), (), s32[]{:S(2)}) async-start(), calls=%async_computation.5 | async-start | bytes 11698176 | tf_op jit(solution)/shard_map/all_gather | solution.py:21
  44.4 463.2 %all-gather.22.cloned.1.call-start = ((), (), s32[]{:S(2)}) async-start(), calls=%async_computation.6 | async-start | bytes 11698176 | tf_op jit(solution)/shard_map/all_gather | solution.py:21
  45.4 2.6 copy-start.4
  45.4 2.7 copy-start.3
  46.7 551.7 %all-gather.24.cloned.1.call-start = ((), (), s32[]{:S(2)}) async-start(), calls=%async_computation.7 | async-start | bytes 11698176 | tf_op jit(solution)/shard_map/all_gather | solution.py:21
  47.4 799.3 %all-reduce.3.cloned.1.call-start = ((), (), s32[]{:S(2)}) async-start(), calls=%async_computation.8 | async-start | bytes 196608
  536.8 32.6 %copy-start.1 = (bf16[8,80,1280]{2,1,0:T(8,128)(2,1)}, bf16[8,80,1280]{2,1,0:T(8,128)(2,1)S(1)}, u32[]{:S(2)}) copy-start(bf16[8,80,1280]{2,1,0:T(8,128)(2,1)S(1)} %get-tuple-element.107) | copy-start | bytes 4915204
  734.6 19.0 %copy-start.5 = (u32[256]{0:T(256)S(1)}, u32[256]{0:T(256)}, u32[]{:S(2)}) copy-start(u32[256]{0:T(256)} %constant.278) | copy-start | bytes 3076
Sparse Core Ops, SparseCore 0:
  27.1 68.9 all-gather.9
  98.0 66.7 all-gather.11
  166.6 66.7 all-gather.13
  235.1 66.7 all-gather.15
  303.7 66.7 all-gather.17
  372.2 66.7 all-gather.19
  440.8 66.7 all-gather.21
  509.5 66.7 all-gather.23
  753.8 92.8 all-reduce.2
